TPU v7x, 32 devices: a whole 2x2x4 slice. The times are simulated.
32 devices in a mesh: section: 2 (over x), dp: 4 (over z), mp: 4 (over y, core).
Axes of the slice: x: 2, y: 2, z: 4, core: 2. Of those that a mesh axis runs over, the one named last changes fastest.
Arguments:
- queries: bfloat16 [2, 4, 640, 4096], P('section', 'dp', None, 'mp')
- keys: bfloat16 [2, 4, 640, 4096], P('section', 'dp', None, 'mp')
- values: bfloat16 [2, 4, 640, 4096], P('section', 'dp', None, 'mp'), may hold values from -6 to 6
- grad_out: bfloat16 [2, 4, 640, 4096], P('section', 'dp', None, 'mp'), may hold values from -6 to 6
- positions: int32 [2, 4, 640], P('section', 'dp'), may hold values from 0 to 319, as said below
Outputs:
- received: bfloat16 [2, 4, 3, 640, 4096], P('section', 'dp', None, 'mp')
- bias_grad: float32 [2, 3, 4096], P('section')
Inputs may be any that keep to these rules, and one draw needn't show every extreme that they name: `positions`: along each sequence a position is 0 or one more than the position before it; the first is 0; a document starts at token 320, and none is longer than 320 tokens.
All inputs are finite; a program needn't handle non-finite values.
Results may differ from a plain program's by a relative error of at most 0.0065.
Values may be sent and summed in bfloat16 or wider, within the bound.
No kernel may reach another device: no remote copies, remote signals or barrier semaphores. Data moves between devices by JAX's collectives and lax.ppermute only.
A program may use at most 64 MiB of HBM per device.

v0:
```python
import math
import jax
import jax.numpy as jnp
from jax import lax
from jax.sharding import PartitionSpec as P

HEAD_DIM = 128
CHUNK_HEADS = 2


def chunk_grads(query_rows, key_rows, value_rows, grad_rows, allowed, halves):
    length, width = query_rows.shape
    heads = width // HEAD_DIM
    block = length // halves
    scaling = 1.0 / math.sqrt(HEAD_DIM)

    def split(rows):
        return rows.reshape(halves, block, heads, HEAD_DIM)

    q, k, v, g = (split(query_rows), split(key_rows), split(value_rows), split(grad_rows))
    scores = jnp.einsum("bqhd,bkhd->bhqk", q, k, preferred_element_type=jnp.float32) * scaling
    scores = jnp.where(allowed[:, None], scores, jnp.float32(-1e30))
    highest = jnp.max(scores, axis=-1, keepdims=True)
    expont = jnp.exp(scores - highest)
    attn = expont / jnp.sum(expont, axis=-1, keepdims=True)
    attn_low = attn.astype(jnp.bfloat16)
    grad_v = jnp.einsum("bhqk,bqhd->bkhd", attn_low, g, preferred_element_type=jnp.float32)
    grad_attn = jnp.einsum("bqhd,bkhd->bhqk", g, v, preferred_element_type=jnp.float32)
    delta = jnp.sum(attn * grad_attn, axis=-1, keepdims=True)
    grad_scores = (attn * (grad_attn - delta) * scaling).astype(jnp.bfloat16)
    grad_q = jnp.einsum("bhqk,bkhd->bqhd", grad_scores, k, preferred_element_type=jnp.float32)
    grad_k = jnp.einsum("bhqk,bqhd->bkhd", grad_scores, q, preferred_element_type=jnp.float32)
    blocks = jnp.stack([grad_q, grad_k, grad_v]).astype(jnp.bfloat16)
    return blocks.reshape(3, length, width)


def per_device(queries, keys, values, grad_out, positions):
    query_rows = queries[0, 0]
    key_rows = keys[0, 0]
    value_rows = values[0, 0]
    grad_rows = grad_out[0, 0]
    token_positions = positions[0, 0]
    length, columns = query_rows.shape
    sections = lax.axis_size("section")
    parts = lax.axis_size("mp")
    replicas = lax.axis_size("dp")
    part = lax.axis_index("mp")
    rows = length // parts
    halves = 2
    block = length // halves
    local = jnp.arange(block, dtype=jnp.int32)
    pos = token_positions.reshape(halves, block)
    allowed = (local[None, None, :] <= local[None, :, None]) & (
        local[None, None, :] >= (local[None, :] - pos)[:, :, None]
    )

    def pairs(shift):
        return [
            ((s + 1) * parts + m, s * parts + (m + shift) % parts)
            for s in range(sections - 1)
            for m in range(parts)
        ]

    width = CHUNK_HEADS * HEAD_DIM
    chunk_count = columns // width
    arrived = [[None] * chunk_count for _ in range(parts)]
    sums = []
    for c in range(chunk_count):
        cols = slice(c * width, (c + 1) * width)
        grads = chunk_grads(
            query_rows[:, cols],
            key_rows[:, cols],
            value_rows[:, cols],
            grad_rows[:, cols],
            allowed,
            halves,
        )
        sums.append(jnp.sum(grads.astype(jnp.float32), axis=1))
        for shift in range(parts):
            target = (part + shift) % parts
            piece = lax.dynamic_slice_in_dim(grads, target * rows, rows, 1)
            arrived[shift][c] = lax.ppermute(piece, ("section", "mp"), pairs(shift))
    own = jnp.concatenate(sums, axis=1)
    slots = lax.dynamic_update_slice_in_dim(
        jnp.zeros((3, columns * parts), jnp.float32), own, part * columns, 1
    )
    totals = lax.psum(slots, ("dp", "mp"))
    totals = lax.ppermute(totals, "section", [(s + 1, s) for s in range(sections - 1)])
    bias_grad = totals / math.sqrt(replicas * length)
    received = jnp.zeros((3, rows, columns * parts), jnp.bfloat16)
    for shift in range(parts):
        source = (part - shift) % parts
        piece = jnp.concatenate(arrived[shift], axis=2)
        received = lax.dynamic_update_slice_in_dim(received, piece, source * columns, 2)
    return (received[None, None], bias_grad[None])


def solution(mesh):
    return jax.shard_map(
        per_device,
        mesh=mesh,
        in_specs=(
            P("section", "dp", None, "mp"),
            P("section", "dp", None, "mp"),
            P("section", "dp", None, "mp"),
            P("section", "dp", None, "mp"),
            P("section", "dp", None),
        ),
        out_specs=(P("section", "dp", None, "mp", None), P("section", None, None)),
        check_vma=False,
    )
```

profile of v0, /device:TPU:5, one launch (start us, length us, event | category | flops | bytes accessed | tf_op | source)
XLA Modules:
  0.0 251.5 jit_solution(15631880437137905530)
XLA Ops:
  0.7 2.3 fusion.237
  5.7 2.2 fusion.239
  10.6 1.5 fusion.135
  12.1 3.2 %fusion.256 = (f32[2,2,320]{2,1,0:T(2,128)S(1)}, f32[2,2,320,320]{2,3,1,0:T(8,128)}) fusion(pred[2,320,320]{1,2,0:T(8,128)(4,1)S(1)} %fusion.124, bf16[2,320,2,128]{3,2,1,0:T(2,128)(2,1)} %reshape.143, bf16[2,320,2,128]{3,2,1,0:T(2,128)(2,1)} %reshape.142), kind=kOutput, calls=%fused_computation.205 | convolution fusion | flops 106496320 | bytes 2503680 | tf_op jit(solution)/shard_map/sub | solution.py:24
  15.3 3.8 %fusion.75 = bf16[2,320,2,128]{3,1,2,0:T(8,128)(2,1)} fusion(f32[2,2,320,320]{2,3,1,0:T(8,128)S(1)} %fusion.135, bf16[2,320,2,128]{3,2,1,0:T(2,128)(2,1)} %reshape.143, f32[2,2,320,320]{2,3,1,0:T(8,128)} %get-tuple-element.41, f32[2,2,320]{2,1,0:T(2,128)S(1)} %get-tuple-element.40), kind=kOutput, calls=%fused_computation.57 | convolution fusion | flops 107890240 | bytes 3937280 | tf_op jit(solution)/shard_map/bhqk,bkhd->bqhd/dot_general | solution.py:31
  19.0 3.6 %fusion.72 = bf16[2,320,2,128]{3,1,2,0:T(8,128)(2,1)} fusion(f32[2,2,320,320]{2,3,1,0:T(8,128)S(1)} %fusion.135, bf16[2,320,2,128]{3,2,1,0:T(2,128)(2,1)} %reshape.142, f32[2,2,320,320]{2,3,1,0:T(8,128)} %get-tuple-element.41, f32[2,2,320]{2,1,0:T(2,128)S(1)} %get-tuple-element.40), kind=kOutput, calls=%fused_computation.56 | convolution fusion | flops 107890240 | bytes 3937280 | tf_op jit(solution)/shard_map/bhqk,bqhd->bkhd/dot_general | solution.py:32
  22.7 2.8 %fusion.96 = bf16[2,320,2,128]{3,1,2,0:T(8,128)(2,1)} fusion(bf16[2,320,2,128]{3,2,1,0:T(2,128)(2,1)} %reshape.144, f32[2,2,320,320]{2,3,1,0:T(8,128)} %get-tuple-element.41, f32[2,2,320]{2,1,0:T(2,128)S(1)} %get-tuple-element.40), kind=kOutput, calls=%fused_computation.64 | convolution fusion | flops 105840640 | bytes 2298880 | tf_op jit(solution)/shard_map/bhqk,bqhd->bkhd/dot_general | solution.py:27
  27.3 2.1 fusion.251
  29.4 1.5 fusion.133
  30.9 3.8 %fusion.81 = bf16[2,320,2,128]{3,1,2,0:T(8,128)(2,1)} fusion(f32[2,2,320,320]{2,3,1,0:T(8,128)S(1)} %fusion.133, bf16[2,320,2,128]{3,2,1,0:T(2,128)(2,1)} %copy-done.22, f32[2,2,320,320]{2,3,1,0:T(8,128)} %get-tuple-element.39, f32[2,2,320]{2,1,0:T(2,128)S(1)} %get-tuple-element.38), kind=kOutput, calls=%fused_computation.59 | convolution fusion | flops 107890240 | bytes 3937280 | tf_op jit(solution)/shard_map/bhqk,bkhd->bqhd/dot_general | solution.py:31
  34.7 3.6 %fusion.78 = bf16[2,320,2,128]{3,1,2,0:T(8,128)(2,1)} fusion(f32[2,2,320,320]{2,3,1,0:T(8,128)S(1)} %fusion.133, bf16[2,320,2,128]{3,2,1,0:T(2,128)(2,1)} %copy-done.20, f32[2,2,320,320]{2,3,1,0:T(8,128)} %get-tuple-element.39, f32[2,2,320]{2,1,0:T(2,128)S(1)} %get-tuple-element.38), kind=kOutput, calls=%fused_computation.58 | convolution fusion | flops 107890240 | bytes 3937280 | tf_op jit(solution)/shard_map/bhqk,bqhd->bkhd/dot_general | solution.py:32
  38.3 2.8 %fusion.97 = bf16[2,320,2,128]{3,1,2,0:T(8,128)(2,1)} fusion(bf16[2,320,2,128]{3,2,1,0:T(2,128)(2,1)} %reshape.148, f32[2,2,320,320]{2,3,1,0:T(8,128)} %get-tuple-element.39, f32[2,2,320]{2,1,0:T(2,128)S(1)} %get-tuple-element.38), kind=kOutput, calls=%fused_computation.65 | convolution fusion | flops 105840640 | bytes 2298880 | tf_op jit(solution)/shard_map/bhqk,bqhd->bkhd/dot_general | solution.py:27
  43.0 2.1 fusion.246
  45.1 1.5 fusion.131
  46.6 3.8 %fusion.87 = bf16[2,320,2,128]{3,1,2,0:T(8,128)(2,1)} fusion(f32[2,2,320,320]{2,3,1,0:T(8,128)S(1)} %fusion.131, bf16[2,320,2,128]{3,2,1,0:T(2,128)(2,1)} %copy-done.23, f32[2,2,320,320]{2,3,1,0:T(8,128)} %get-tuple-element.37, f32[2,2,320]{2,1,0:T(2,128)S(1)} %get-tuple-element.36), kind=kOutput, calls=%fused_computation.61 | convolution fusion | flops 107890240 | bytes 3937280 | tf_op jit(solution)/shard_map/bhqk,bkhd->bqhd/dot_general | solution.py:31
  50.4 3.6 %fusion.84 = bf16[2,320,2,128]{3,1,2,0:T(8,128)(2,1)} fusion(f32[2,2,320,320]{2,3,1,0:T(8,128)S(1)} %fusion.131, bf16[2,320,2,128]{3,2,1,0:T(2,128)(2,1)} %copy-done.21, f32[2,2,320,320]{2,3,1,0:T(8,128)} %get-tuple-element.37, f32[2,2,320]{2,1,0:T(2,128)S(1)} %get-tuple-element.36), kind=kOutput, calls=%fused_computation.60 | convolution fusion | flops 107890240 | bytes 3937280 | tf_op jit(solution)/shard_map/bhqk,bqhd->bkhd/dot_general | solution.py:32
  54.0 2.7 %fusion.98 = bf16[2,320,2,128]{3,1,2,0:T(8,128)(2,1)} fusion(bf16[2,320,2,128]{3,2,1,0:T(2,128)(2,1)} %reshape.152, f32[2,2,320,320]{2,3,1,0:T(8,128)} %get-tuple-element.37, f32[2,2,320]{2,1,0:T(2,128)S(1)} %get-tuple-element.36), kind=kOutput, calls=%fused_computation.66 | convolution fusion | flops 105840640 | bytes 2298880 | tf_op jit(solution)/shard_map/bhqk,bqhd->bkhd/dot_general | solution.py:27
  57.0 2.3 fusion.241
  59.8 3.6 %fusion.90 = bf16[2,320,2,128]{3,1,2,0:T(8,128)(2,1)} fusion(f32[2,2,320,320]{2,3,1,0:T(8,128)S(1)} %fusion.129, bf16[2,320,2,128]{3,2,1,0:T(2,128)(2,1)S(1)} %reshape.154, f32[2,2,320,320]{2,3,1,0:T(8,128)} %get-tuple-element.35, f32[2,2,320]{2,1,0:T(2,128)S(1)} %get-tuple-element.34), kind=kOutput, calls=%fused_computation.62 | convolution fusion | flops 107890240 | bytes 3937280 | tf_op jit(solution)/shard_map/bhqk,bqhd->bkhd/dot_general | solution.py:32
  63.4 3.7 %fusion.93 = bf16[2,320,2,128]{3,1,2,0:T(8,128)(2,1)} fusion(f32[2,2,320,320]{2,3,1,0:T(8,128)S(1)} %fusion.129, bf16[2,320,2,128]{3,2,1,0:T(2,128)(2,1)S(1)} %reshape.155, f32[2,2,320,320]{2,3,1,0:T(8,128)} %get-tuple-element.35, f32[2,2,320]{2,1,0:T(2,128)S(1)} %get-tuple-element.34), kind=kOutput, calls=%fused_computation.63 | convolution fusion | flops 107890240 | bytes 3937280 | tf_op jit(solution)/shard_map/bhqk,bkhd->bqhd/dot_general | solution.py:31
  67.1 2.7 %fusion.99 = bf16[2,320,2,128]{3,1,2,0:T(8,128)(2,1)} fusion(bf16[2,320,2,128]{3,2,1,0:T(2,128)(2,1)S(1)} %reshape.156, f32[2,2,320,320]{2,3,1,0:T(8,128)} %get-tuple-element.35, f32[2,2,320]{2,1,0:T(2,128)S(1)} %get-tuple-element.34), kind=kOutput, calls=%fused_computation.67 | convolution fusion | flops 105840640 | bytes 2298880 | tf_op jit(solution)/shard_map/bhqk,bqhd->bkhd/dot_general | solution.py:27
  75.5 2.0 copy.41
  78.7 2.0 copy.43
  80.7 1.9 stack.58
  86.1 2.0 copy.50
  88.2 1.9 stack.60
  90.1 1.7 constant_dynamic-update-slice_fusion.11
  91.8 2.0 copy.54
  93.8 1.9 stack.62
  96.4 1.7 constant_dynamic-update-slice_fusion.9
  99.6 53.4 %psum.7 = f32[3,4096]{1,0:T(4,128)} all-reduce(f32[3,4096]{1,0:T(4,128)S(1)} %maximum_dynamic-update-slice_fusion), channel_id=1, replica_groups=mesh['section'=2,'dp'=4,'mp'=4] {'dp','mp'}, use_global_device_ids=true, to_apply=%region_16.17 | all-reduce | flops 12288 | bytes 98304 | tf_op jit(solution)/shard_map/psum | solution.py:87
  155.1 1.4 collective-permute-start
  157.4 1.4 collective-permute-start.1
  165.9 1.5 collective-permute-done.1
  168.7 4.0 %collective-permute-done.2 = bf16[3,160,256]{2,1,0:T(8,128)(2,1)S(1)} collective-permute-done((bf16[3,160,256]{2,1,0:T(8,128)(2,1)}, bf16[3,160,256]{2,1,0:T(8,128)(2,1)S(1)}, u32[]{:S(2)}, u32[]{:S(2)}) %collective-permute-start.2) | collective-permute-done | bytes 245792 | tf_op jit(solution)/shard_map/ppermute | solution.py:82
  174.0 3.9 %collective-permute-done.3 = bf16[3,160,256]{2,1,0:T(8,128)(2,1)S(1)} collective-permute-done((bf16[3,160,256]{2,1,0:T(8,128)(2,1)}, bf16[3,160,256]{2,1,0:T(8,128)(2,1)S(1)}, u32[]{:S(2)}, u32[]{:S(2)}) %collective-permute-start.3) | collective-permute-done | bytes 245792 | tf_op jit(solution)/shard_map/ppermute | solution.py:82
  179.1 12.5 %collective-permute-done.4 = bf16[3,160,256]{2,1,0:T(8,128)(2,1)S(1)} collective-permute-done((bf16[3,160,256]{2,1,0:T(8,128)(2,1)}, bf16[3,160,256]{2,1,0:T(8,128)(2,1)S(1)}, u32[]{:S(2)}, u32[]{:S(2)}) %collective-permute-start.4) | collective-permute-done | bytes 245792 | tf_op jit(solution)/shard_map/ppermute | solution.py:82
  193.0 4.0 %collective-permute-done.5 = bf16[3,160,256]{2,1,0:T(8,128)(2,1)S(1)} collective-permute-done((bf16[3,160,256]{2,1,0:T(8,128)(2,1)}, bf16[3,160,256]{2,1,0:T(8,128)(2,1)S(1)}, u32[]{:S(2)}, u32[]{:S(2)}) %collective-permute-start.5) | collective-permute-done | bytes 245792 | tf_op jit(solution)/shard_map/ppermute | solution.py:82
  198.9 3.3 %collective-permute-done.6 = bf16[3,160,256]{2,1,0:T(8,128)(2,1)S(1)} collective-permute-done((bf16[3,160,256]{2,1,0:T(8,128)(2,1)S(1)}, bf16[3,160,256]{2,1,0:T(8,128)(2,1)S(1)}, u32[]{:S(2)}, u32[]{:S(2)}) %collective-permute-start.6) | collective-permute-done | bytes 245792 | tf_op jit(solution)/shard_map/ppermute | solution.py:82
  205.1 2.0 collective-permute-done.7
  209.8 4.1 %collective-permute-done.9 = bf16[3,160,256]{2,1,0:T(8,128)(2,1)S(1)} collective-permute-done((bf16[3,160,256]{2,1,0:T(8,128)(2,1)S(1)}, bf16[3,160,256]{2,1,0:T(8,128)(2,1)S(1)}, u32[]{:S(2)}, u32[]{:S(2)}) %collective-permute-start.9) | collective-permute-done | bytes 245792 | tf_op jit(solution)/shard_map/ppermute | solution.py:82
  215.1 4.0 %collective-permute-done.10 = bf16[3,160,256]{2,1,0:T(8,128)(2,1)S(1)} collective-permute-done((bf16[3,160,256]{2,1,0:T(8,128)(2,1)S(1)}, bf16[3,160,256]{2,1,0:T(8,128)(2,1)S(1)}, u32[]{:S(2)}, u32[]{:S(2)}) %collective-permute-start.10) | collective-permute-done | bytes 245792 | tf_op jit(solution)/shard_map/ppermute | solution.py:82
  220.5 3.9 %collective-permute-done.11 = bf16[3,160,256]{2,1,0:T(8,128)(2,1)S(1)} collective-permute-done((bf16[3,160,256]{2,1,0:T(8,128)(2,1)S(1)}, bf16[3,160,256]{2,1,0:T(8,128)(2,1)S(1)}, u32[]{:S(2)}, u32[]{:S(2)}) %collective-permute-start.11) | collective-permute-done | bytes 245792 | tf_op jit(solution)/shard_map/ppermute | solution.py:82
  224.5 13.4 %collective-permute-done.12 = bf16[3,160,256]{2,1,0:T(8,128)(2,1)S(1)} collective-permute-done((bf16[3,160,256]{2,1,0:T(8,128)(2,1)S(1)}, bf16[3,160,256]{2,1,0:T(8,128)(2,1)S(1)}, u32[]{:S(2)}, u32[]{:S(2)}) %collective-permute-start.12) | collective-permute-done | bytes 245792 | tf_op jit(solution)/shard_map/ppermute | solution.py:82
  237.9 5.3 %collective-permute-done.13 = bf16[3,160,256]{2,1,0:T(8,128)(2,1)S(1)} collective-permute-done((bf16[3,160,256]{2,1,0:T(8,128)(2,1)S(1)}, bf16[3,160,256]{2,1,0:T(8,128)(2,1)S(1)}, u32[]{:S(2)}, u32[]{:S(2)}) %collective-permute-start.13) | collective-permute-done | bytes 245792 | tf_op jit(solution)/shard_map/ppermute | solution.py:82
  243.2 3.6 %collective-permute-done.14 = bf16[3,160,256]{2,1,0:T(8,128)(2,1)S(1)} collective-permute-done((bf16[3,160,256]{2,1,0:T(8,128)(2,1)S(1)}, bf16[3,160,256]{2,1,0:T(8,128)(2,1)S(1)}, u32[]{:S(2)}, u32[]{:S(2)}) %collective-permute-start.14) | collective-permute-done | bytes 245792 | tf_op jit(solution)/shard_map/ppermute | solution.py:82
  246.8 2.6 %collective-permute-done.15 = bf16[3,160,256]{2,1,0:T(8,128)(2,1)S(1)} collective-permute-done((bf16[3,160,256]{2,1,0:T(8,128)(2,1)S(1)}, bf16[3,160,256]{2,1,0:T(8,128)(2,1)S(1)}, u32[]{:S(2)}, u32[]{:S(2)}) %collective-permute-start.15) | collective-permute-done | bytes 245792 | tf_op jit(solution)/shard_map/ppermute | solution.py:82
  249.6 1.9 copy-done.1
  (139 shorter events, 47.4 us)
Async XLA Ops:
  0.6 3.2 %copy-start.10 = (bf16[1,1,640,1024]{3,2,1,0:T(8,128)(2,1)S(1)}, bf16[1,1,640,1024]{3,2,1,0:T(8,128)(2,1)}, u32[]{:S(2)}) copy-start(bf16[1,1,640,1024]{3,2,1,0:T(8,128)(2,1)} %param.6) | copy-start | bytes 3932164
  3.0 2.5 %copy-start.26 = (s32[1,1,640]{2,1,0:T(1,128)S(1)}, s32[1,1,640]{2,1,0:T(1,128)}, u32[]{:S(2)}) copy-start(s32[1,1,640]{2,1,0:T(1,128)} %param.9) | copy-start | bytes 7684
  4.8 3.9 %copy-start.11 = (bf16[1,1,640,1024]{3,2,1,0:T(8,128)(2,1)S(1)}, bf16[1,1,640,1024]{3,2,1,0:T(8,128)(2,1)}, u32[]{:S(2)}) copy-start(bf16[1,1,640,1024]{3,2,1,0:T(8,128)(2,1)} %param.7) | copy-start | bytes 3932164
  22.7 2.8 %copy-start.6 = (bf16[640,256]{1,0:T(8,128)(2,1)S(1)}, bf16[640,256]{1,0:T(8,128)(2,1)}, u32[]{:S(2)}) copy-start(bf16[640,256]{1,0:T(8,128)(2,1)} %get-tuple-element.5) | copy-start | bytes 983044
  22.7 2.9 %copy-start.7 = (bf16[640,256]{1,0:T(8,128)(2,1)S(1)}, bf16[640,256]{1,0:T(8,128)(2,1)}, u32[]{:S(2)}) copy-start(bf16[640,256]{1,0:T(8,128)(2,1)} %get-tuple-element.9) | copy-start | bytes 983044
  22.7 3.0 %copy-start.8 = (bf16[640,256]{1,0:T(8,128)(2,1)S(1)}, bf16[640,256]{1,0:T(8,128)(2,1)}, u32[]{:S(2)}) copy-start(bf16[640,256]{1,0:T(8,128)(2,1)} %get-tuple-element.13) | copy-start | bytes 983044
  25.5 1.0 copy-start.9
  25.5 1.7 copy-start.20
  25.7 1.6 copy-start.22
  38.3 2.8 %copy-start.2 = (bf16[640,256]{1,0:T(8,128)(2,1)S(1)}, bf16[640,256]{1,0:T(8,128)(2,1)}, u32[]{:S(2)}) copy-start(bf16[640,256]{1,0:T(8,128)(2,1)} %get-tuple-element.4) | copy-start | bytes 983044
  38.3 2.9 %copy-start.3 = (bf16[640,256]{1,0:T(8,128)(2,1)S(1)}, bf16[640,256]{1,0:T(8,128)(2,1)}, u32[]{:S(2)}) copy-start(bf16[640,256]{1,0:T(8,128)(2,1)} %get-tuple-element.8) | copy-start | bytes 983044
  38.3 3.0 %copy-start.4 = (bf16[640,256]{1,0:T(8,128)(2,1)S(1)}, bf16[640,256]{1,0:T(8,128)(2,1)}, u32[]{:S(2)}) copy-start(bf16[640,256]{1,0:T(8,128)(2,1)} %get-tuple-element.12) | copy-start | bytes 983044
  41.1 1.0 copy-start.5
  41.2 1.8 copy-start.21
  41.3 1.7 copy-start.23
  67.1 2.7 %copy-start.16 = (bf16[2,320,2,128]{3,1,2,0:T(8,128)(2,1)S(1)}, bf16[2,320,2,128]{3,1,2,0:T(8,128)(2,1)}, u32[]{:S(2)}) copy-start(bf16[2,320,2,128]{3,1,2,0:T(8,128)(2,1)} %fusion.75) | copy-start | bytes 983044
  69.8 1.0 copy-start.13
  69.8 1.5 copy-start.12
  71.4 1.0 copy-start.17
  72.0 1.0 copy-start.15
  72.0 1.5 copy-start.14
  73.9 1.0 copy-start.18
  82.6 1.2 copy-start.19
  152.9 10.2 %collective-permute-start.16 = (f32[3,4096]{1,0:T(4,128)}, f32[3,4096]{1,0:T(4,128)S(1)}, u32[]{:S(2)}, u32[]{:S(2)}) collective-permute-start(f32[3,4096]{1,0:T(4,128)} %psum.7), channel_id=1, source_target_pairs={{16,0},{17,1},{18,2},{19,3},{20,4},{21,5},{22,6},{23,7},{24,8},{25... | collective-permute-start | bytes 147464 | tf_op jit(solution)/shard_map/ppermute | solution.py:88
  155.1 6.0 %copy-start = (bf16[3,640,256]{2,1,0:T(8,128)(2,1)S(1)}, bf16[3,640,256]{2,1,0:T(8,128)(2,1)}, u32[]{:S(2)}) copy-start(bf16[3,640,256]{2,1,0:T(8,128)(2,1)} %constant_dynamic-update-slice_fusion.9) | copy-start | bytes 2949124
  155.1 9.4 %collective-permute-start = (bf16[3,160,256]{2,1,0:T(8,128)(2,1)S(1)}, bf16[3,160,256]{2,1,0:T(8,128)(2,1)}, u32[]{:S(2)}, u32[]{:S(2)}) collective-permute-start(bf16[3,160,256]{2,1,0:T(8,128)(2,1)S(1)} %get-tuple-element.21), channel_id=1, source_target_pairs={{16,0},{17,1},{18,2},{19,3},{20,4},{21,5},{22,6},{23,7},{24,8},{25... | collective-permute-start | bytes 737288 | tf_op jit(solution)/shard_map/ppermute | solution.py:82
  157.4 34.3 %copy-start.24 = (bf16[3,160,256]{2,1,0:T(8,128)(2,1)S(1)}, bf16[3,160,256]{2,1,0:T(8,128)(2,1)}, u32[]{:S(2)}) copy-start(bf16[3,160,256]{2,1,0:T(8,128)(2,1)} %get-tuple-element.23) | copy-start | bytes 737284
  157.4 10.0 %collective-permute-start.1 = (bf16[3,160,256]{2,1,0:T(8,128)(2,1)}, bf16[3,160,256]{2,1,0:T(8,128)(2,1)}, u32[]{:S(2)}, u32[]{:S(2)}) collective-permute-start(bf16[3,160,256]{2,1,0:T(8,128)(2,1)} %get-tuple-element.25), channel_id=1, source_target_pairs={{16,0},{17,1},{18,2},{19,3},{20,4},{21,5},{22,6},{23,7},{24,8},{25... | collective-permute-start | bytes 737288 | tf_op jit(solution)/shard_map/ppermute | solution.py:82
  159.7 7.7 %copy-start.25 = (bf16[3,160,256]{2,1,0:T(8,128)(2,1)S(1)}, bf16[3,160,256]{2,1,0:T(8,128)(2,1)}, u32[]{:S(2)}) copy-start(bf16[3,160,256]{2,1,0:T(8,128)(2,1)} %get-tuple-element.28) | copy-start | bytes 737284
  159.7 13.0 %collective-permute-start.2 = (bf16[3,160,256]{2,1,0:T(8,128)(2,1)}, bf16[3,160,256]{2,1,0:T(8,128)(2,1)S(1)}, u32[]{:S(2)}, u32[]{:S(2)}) collective-permute-start(bf16[3,160,256]{2,1,0:T(8,128)(2,1)} %get-tuple-element.29), channel_id=1, source_target_pairs={{16,0},{17,1},{18,2},{19,3},{20,4},{21,5},{22,6},{23,7},{24,8},{25... | collective-permute-start | bytes 737288 | tf_op jit(solution)/shard_map/ppermute | solution.py:82
  161.9 16.0 %collective-permute-start.3 = (bf16[3,160,256]{2,1,0:T(8,128)(2,1)}, bf16[3,160,256]{2,1,0:T(8,128)(2,1)S(1)}, u32[]{:S(2)}, u32[]{:S(2)}) collective-permute-start(bf16[3,160,256]{2,1,0:T(8,128)(2,1)} %get-tuple-element.33), channel_id=1, source_target_pairs={{16,0},{17,1},{18,2},{19,3},{20,4},{21,5},{22,6},{23,7},{24,8},{25... | collective-permute-start | bytes 737288 | tf_op jit(solution)/shard_map/ppermute | solution.py:82
  163.2 28.5 %collective-permute-start.4 = (bf16[3,160,256]{2,1,0:T(8,128)(2,1)}, bf16[3,160,256]{2,1,0:T(8,128)(2,1)S(1)}, u32[]{:S(2)}, u32[]{:S(2)}) collective-permute-start(bf16[3,160,256]{2,1,0:T(8,128)(2,1)} %get-tuple-element.20), channel_id=1, source_target_pairs={{16,1},{17,2},{18,3},{19,0},{20,5},{21,6},{22,7},{23,4},{24,9},{25... | collective-permute-start | bytes 737288 | tf_op jit(solution)/shard_map/ppermute | solution.py:82
  164.5 32.4 %collective-permute-start.5 = (bf16[3,160,256]{2,1,0:T(8,128)(2,1)}, bf16[3,160,256]{2,1,0:T(8,128)(2,1)S(1)}, u32[]{:S(2)}, u32[]{:S(2)}) collective-permute-start(bf16[3,160,256]{2,1,0:T(8,128)(2,1)} %get-tuple-element.24), channel_id=1, source_target_pairs={{16,1},{17,2},{18,3},{19,0},{20,5},{21,6},{22,7},{23,4},{24,9},{25... | collective-permute-start | bytes 737288 | tf_op jit(solution)/shard_map/ppermute | solution.py:82
  167.4 34.8 %collective-permute-start.6 = (bf16[3,160,256]{2,1,0:T(8,128)(2,1)S(1)}, bf16[3,160,256]{2,1,0:T(8,128)(2,1)S(1)}, u32[]{:S(2)}, u32[]{:S(2)}) collective-permute-start(bf16[3,160,256]{2,1,0:T(8,128)(2,1)S(1)} %copy-done.25), channel_id=1, source_target_pairs={{16,1},{17,2},{18,3},{19,0},{20,5},{21,6},{22,7},{23,4},{24,9},{25... | collective-permute-start | bytes 737288 | tf_op jit(solution)/shard_map/ppermute | solution.py:82
  172.7 34.5 %collective-permute-start.7 = (bf16[3,160,256]{2,1,0:T(8,128)(2,1)S(1)}, bf16[3,160,256]{2,1,0:T(8,128)(2,1)S(1)}, u32[]{:S(2)}, u32[]{:S(2)}) collective-permute-start(bf16[3,160,256]{2,1,0:T(8,128)(2,1)S(1)} %get-tuple-element.32), channel_id=1, source_target_pairs={{16,1},{17,2},{18,3},{19,0},{20,5},{21,6},{22,7},{23,4},{24,9},{25... | collective-permute-start | bytes 737288 | tf_op jit(solution)/shard_map/ppermute | solution.py:82
  177.8 30.6 %collective-permute-start.8 = (bf16[3,160,256]{2,1,0:T(8,128)(2,1)S(1)}, bf16[3,160,256]{2,1,0:T(8,128)(2,1)S(1)}, u32[]{:S(2)}, u32[]{:S(2)}) collective-permute-start(bf16[3,160,256]{2,1,0:T(8,128)(2,1)S(1)} %get-tuple-element.19), channel_id=1, source_target_pairs={{16,2},{17,3},{18,0},{19,1},{20,6},{21,7},{22,4},{23,5},{24,10},{2... | collective-permute-start | bytes 737288 | tf_op jit(solution)/shard_map/ppermute | solution.py:82
  191.7 22.2 %collective-permute-start.9 = (bf16[3,160,256]{2,1,0:T(8,128)(2,1)S(1)}, bf16[3,160,256]{2,1,0:T(8,128)(2,1)S(1)}, u32[]{:S(2)}, u32[]{:S(2)}) collective-permute-start(bf16[3,160,256]{2,1,0:T(8,128)(2,1)S(1)} %copy-done.24), channel_id=1, source_target_pairs={{16,2},{17,3},{18,0},{19,1},{20,6},{21,7},{22,4},{23,5},{24,10},{2... | collective-permute-start | bytes 737288 | tf_op jit(solution)/shard_map/ppermute | solution.py:82
  196.9 22.2 %collective-permute-start.10 = (bf16[3,160,256]{2,1,0:T(8,128)(2,1)S(1)}, bf16[3,160,256]{2,1,0:T(8,128)(2,1)S(1)}, u32[]{:S(2)}, u32[]{:S(2)}) collective-permute-start(bf16[3,160,256]{2,1,0:T(8,128)(2,1)S(1)} %get-tuple-element.27), channel_id=1, source_target_pairs={{16,2},{17,3},{18,0},{19,1},{20,6},{21,7},{22,4},{23,5},{24,10},{2... | collective-permute-start | bytes 737288 | tf_op jit(solution)/shard_map/ppermute | solution.py:82
  202.2 22.2 %collective-permute-start.11 = (bf16[3,160,256]{2,1,0:T(8,128)(2,1)S(1)}, bf16[3,160,256]{2,1,0:T(8,128)(2,1)S(1)}, u32[]{:S(2)}, u32[]{:S(2)}) collective-permute-start(bf16[3,160,256]{2,1,0:T(8,128)(2,1)S(1)} %get-tuple-element.31), channel_id=1, source_target_pairs={{16,2},{17,3},{18,0},{19,1},{20,6},{21,7},{22,4},{23,5},{24,10},{2... | collective-permute-start | bytes 737288 | tf_op jit(solution)/shard_map/ppermute | solution.py:82
  207.2 30.7 %collective-permute-start.12 = (bf16[3,160,256]{2,1,0:T(8,128)(2,1)S(1)}, bf16[3,160,256]{2,1,0:T(8,128)(2,1)S(1)}, u32[]{:S(2)}, u32[]{:S(2)}) collective-permute-start(bf16[3,160,256]{2,1,0:T(8,128)(2,1)S(1)} %get-tuple-element.18), channel_id=1, source_target_pairs={{16,3},{17,0},{18,1},{19,2},{20,7},{21,4},{22,5},{23,6},{24,11},{2... | collective-permute-start | bytes 737288 | tf_op jit(solution)/shard_map/ppermute | solution.py:82
  208.5 34.7 %collective-permute-start.13 = (bf16[3,160,256]{2,1,0:T(8,128)(2,1)S(1)}, bf16[3,160,256]{2,1,0:T(8,128)(2,1)S(1)}, u32[]{:S(2)}, u32[]{:S(2)}) collective-permute-start(bf16[3,160,256]{2,1,0:T(8,128)(2,1)S(1)} %get-tuple-element.22), channel_id=1, source_target_pairs={{16,3},{17,0},{18,1},{19,2},{20,7},{21,4},{22,5},{23,6},{24,11},{2... | collective-permute-start | bytes 737288 | tf_op jit(solution)/shard_map/ppermute | solution.py:82
  213.8 33.0 %collective-permute-start.14 = (bf16[3,160,256]{2,1,0:T(8,128)(2,1)S(1)}, bf16[3,160,256]{2,1,0:T(8,128)(2,1)S(1)}, u32[]{:S(2)}, u32[]{:S(2)}) collective-permute-start(bf16[3,160,256]{2,1,0:T(8,128)(2,1)S(1)} %get-tuple-element.26), channel_id=1, source_target_pairs={{16,3},{17,0},{18,1},{19,2},{20,7},{21,4},{22,5},{23,6},{24,11},{2... | collective-permute-start | bytes 737288 | tf_op jit(solution)/shard_map/ppermute | solution.py:82
  219.1 30.3 %collective-permute-start.15 = (bf16[3,160,256]{2,1,0:T(8,128)(2,1)S(1)}, bf16[3,160,256]{2,1,0:T(8,128)(2,1)S(1)}, u32[]{:S(2)}, u32[]{:S(2)}) collective-permute-start(bf16[3,160,256]{2,1,0:T(8,128)(2,1)S(1)} %get-tuple-element.30), channel_id=1, source_target_pairs={{16,3},{17,0},{18,1},{19,2},{20,7},{21,4},{22,5},{23,6},{24,11},{2... | collective-permute-start | bytes 737288 | tf_op jit(solution)/shard_map/ppermute | solution.py:82
  249.5 1.9 copy-start.1
where the time goes:
time: 253 us; the launch traced here: 251 us
  waiting for transfers between devices  68.1 us (27%)
  matrix products  55.1 us (22%)
  blocking collectives  53.4 us (21%)
  local copies, waits for them, and re-layouts  47.7 us (19%)
  starting transfers between devices  22.2 us (9%)
  other arithmetic  3.64 us (1%)
    ppermute x16, waiting for transfers between devices, per_device(): arrived[shift][c] = lax.ppermute(piece, ('section', 'mp'), pairs(shift))  68.1 us
    psum x1, blocking collectives, per_device(): totals = lax.psum(slots, ('dp', 'mp'))  53.4 us
    ppermute x16, starting transfers between devices, per_device(): arrived[shift][c] = lax.ppermute(piece, ('section', 'mp'), pairs(shift))  20.9 us
    dot_general x4, matrix products, chunk_grads(): jnp.einsum('bhqk,bkhd->bqhd', grad_scores, k, preferred_element_type=jnp....  15.1 us
    dot_general x4, matrix products, chunk_grads(): jnp.einsum('bhqk,bqhd->bkhd', grad_scores, q, preferred_element_type=jnp....  14.5 us
    another operation x16, local copies, waits for them, and re-layouts, chunk_grads(): blocks = jnp.stack([grad_q, grad_k, grad_v]).astype(jnp.bfloat16)  12.4 us
    dot_general x4, matrix products, chunk_grads(): jnp.einsum('bhqk,bqhd->bkhd', attn_low, g, preferred_element_type=jnp.flo...  11 us
    sub x4, matrix products, chunk_grads(): expont = jnp.exp(scores - highest)  9.71 us
  transfers between devices with their start and end apart: 17, of which 14 were waited for; matrix products, arithmetic and copies ran while one was open for 2% of the time, Pallas kernels for 0%

commit v1 on v0

--- a/solution.py
+++ b/solution.py
@@ -84,7 +84,7 @@
     slots = lax.dynamic_update_slice_in_dim(
         jnp.zeros((3, columns * parts), jnp.float32), own, part * columns, 1
     )
-    totals = lax.psum(slots, ("dp", "mp"))
+    totals = jax.lax.all_gather(slots, ("dp", "mp")).sum(axis=0)
     totals = lax.ppermute(totals, "section", [(s + 1, s) for s in range(sections - 1)])
     bias_grad = totals / math.sqrt(replicas * length)
     received = jnp.zeros((3, rows, columns * parts), jnp.bfloat16)

time: 253 us -> 223 us (0.88)
  blocking collectives: 53.4 us -> 22.9 us
    psum x1 -> x0, blocking collectives: 53.4 us -> none  [per_device(): totals = lax.psum(slots, ('dp', 'mp'))]
    all_gather x0 -> x1, blocking collectives: none -> 22.9 us  [per_device(): totals = jax.lax.all_gather(slots, ('dp', 'mp')).sum(axis=0)]
  transfers between devices with their start and end apart: 17 -> 17, of which waited for: 14 -> 16; matrix products, arithmetic and copies ran while one was open for 2% -> 3% of each run, Pallas kernels for 0% -> 0%
where the time goes in v1:
time: 223 us; the launch traced here: 221 us
  waiting for transfers between devices  65.8 us (30%)
  matrix products  55.1 us (25%)
  local copies, waits for them, and re-layouts  47.7 us (21%)
  blocking collectives  22.9 us (10%)
  starting transfers between devices  22.2 us (10%)
  other arithmetic  5.87 us (3%)
    ppermute x16, waiting for transfers between devices, per_device(): arrived[shift][c] = lax.ppermute(piece, ('section', 'mp'), pairs(shift))  65.7 us
    all_gather x1, blocking collectives, per_device(): totals = jax.lax.all_gather(slots, ('dp', 'mp')).sum(axis=0)  22.9 us
    ppermute x16, starting transfers between devices, per_device(): arrived[shift][c] = lax.ppermute(piece, ('section', 'mp'), pairs(shift))  20.9 us
    dot_general x4, matrix products, chunk_grads(): jnp.einsum('bhqk,bkhd->bqhd', grad_scores, k, preferred_element_type=jnp....  15.1 us
    dot_general x4, matrix products, chunk_grads(): jnp.einsum('bhqk,bqhd->bkhd', grad_scores, q, preferred_element_type=jnp....  14.5 us
    another operation x16, local copies, waits for them, and re-layouts, chunk_grads(): blocks = jnp.stack([grad_q, grad_k, grad_v]).astype(jnp.bfloat16)  12.4 us
    dot_general x4, matrix products, chunk_grads(): jnp.einsum('bhqk,bqhd->bkhd', attn_low, g, preferred_element_type=jnp.flo...  11 us
    sub x4, matrix products, chunk_grads(): expont = jnp.exp(scores - highest)  9.71 us
  transfers between devices with their start and end apart: 17, of which 16 were waited for; matrix products, arithmetic and copies ran while one was open for 3% of the time, Pallas kernels for 0%

profile of v1, /device:TPU:5, one launch (start us, length us, event | category | flops | bytes accessed | tf_op | source)
XLA Modules:
  0.0 220.9 jit_solution(6214539981801723096)
XLA Ops:
  0.7 2.3 %fusion.238 = (bf16[640,256]{1,0:T(8,128)(2,1)S(1)}, bf16[640,256]{1,0:T(8,128)(2,1)S(1)}, bf16[640,256]{1,0:T(8,128)(2,1)}, bf16[640,256]{1,0:T(8,128)(2,1)}) fusion(bf16[640,1024]{1,0:T(8,128)(2,1)} %bitcast.48), kind=kLoop, calls=%fused_computation.199 | loop fusion | bytes 2621440 | tf_op jit(solution)/shard_map/slice | solution.py:71
  5.7 2.2 %fusion.240 = (bf16[640,256]{1,0:T(8,128)(2,1)S(1)}, bf16[640,256]{1,0:T(8,128)(2,1)S(1)}, bf16[640,256]{1,0:T(8,128)(2,1)}, bf16[640,256]{1,0:T(8,128)(2,1)}) fusion(bf16[640,1024]{1,0:T(8,128)(2,1)} %bitcast.50), kind=kLoop, calls=%fused_computation.201 | loop fusion | bytes 2621440 | tf_op jit(solution)/shard_map/slice | solution.py:74
  10.6 1.5 fusion.135
  12.1 3.2 %fusion.257 = (f32[2,2,320]{2,1,0:T(2,128)S(1)}, f32[2,2,320,320]{2,3,1,0:T(8,128)}) fusion(pred[2,320,320]{1,2,0:T(8,128)(4,1)S(1)} %fusion.124, bf16[2,320,2,128]{3,2,1,0:T(2,128)(2,1)} %reshape.145, bf16[2,320,2,128]{3,2,1,0:T(2,128)(2,1)} %reshape.144), kind=kOutput, calls=%fused_computation.206 | convolution fusion | flops 106496320 | bytes 2503680 | tf_op jit(solution)/shard_map/sub | solution.py:24
  15.3 3.8 %fusion.75 = bf16[2,320,2,128]{3,1,2,0:T(8,128)(2,1)} fusion(f32[2,2,320,320]{2,3,1,0:T(8,128)S(1)} %fusion.135, bf16[2,320,2,128]{3,2,1,0:T(2,128)(2,1)} %reshape.145, f32[2,2,320,320]{2,3,1,0:T(8,128)} %get-tuple-element.41, f32[2,2,320]{2,1,0:T(2,128)S(1)} %get-tuple-element.40), kind=kOutput, calls=%fused_computation.57 | convolution fusion | flops 107890240 | bytes 3937280 | tf_op jit(solution)/shard_map/bhqk,bkhd->bqhd/dot_general | solution.py:31
  19.0 3.6 %fusion.72 = bf16[2,320,2,128]{3,1,2,0:T(8,128)(2,1)} fusion(f32[2,2,320,320]{2,3,1,0:T(8,128)S(1)} %fusion.135, bf16[2,320,2,128]{3,2,1,0:T(2,128)(2,1)} %reshape.144, f32[2,2,320,320]{2,3,1,0:T(8,128)} %get-tuple-element.41, f32[2,2,320]{2,1,0:T(2,128)S(1)} %get-tuple-element.40), kind=kOutput, calls=%fused_computation.56 | convolution fusion | flops 107890240 | bytes 3937280 | tf_op jit(solution)/shard_map/bhqk,bqhd->bkhd/dot_general | solution.py:32
  22.7 2.8 %fusion.96 = bf16[2,320,2,128]{3,1,2,0:T(8,128)(2,1)} fusion(bf16[2,320,2,128]{3,2,1,0:T(2,128)(2,1)} %reshape.146, f32[2,2,320,320]{2,3,1,0:T(8,128)} %get-tuple-element.41, f32[2,2,320]{2,1,0:T(2,128)S(1)} %get-tuple-element.40), kind=kOutput, calls=%fused_computation.64 | convolution fusion | flops 105840640 | bytes 2298880 | tf_op jit(solution)/shard_map/bhqk,bqhd->bkhd/dot_general | solution.py:27
  27.3 2.1 fusion.252
  29.4 1.5 fusion.133
  30.9 3.8 %fusion.81 = bf16[2,320,2,128]{3,1,2,0:T(8,128)(2,1)} fusion(f32[2,2,320,320]{2,3,1,0:T(8,128)S(1)} %fusion.133, bf16[2,320,2,128]{3,2,1,0:T(2,128)(2,1)} %copy-done.22, f32[2,2,320,320]{2,3,1,0:T(8,128)} %get-tuple-element.39, f32[2,2,320]{2,1,0:T(2,128)S(1)} %get-tuple-element.38), kind=kOutput, calls=%fused_computation.59 | convolution fusion | flops 107890240 | bytes 3937280 | tf_op jit(solution)/shard_map/bhqk,bkhd->bqhd/dot_general | solution.py:31
  34.7 3.6 %fusion.78 = bf16[2,320,2,128]{3,1,2,0:T(8,128)(2,1)} fusion(f32[2,2,320,320]{2,3,1,0:T(8,128)S(1)} %fusion.133, bf16[2,320,2,128]{3,2,1,0:T(2,128)(2,1)} %copy-done.20, f32[2,2,320,320]{2,3,1,0:T(8,128)} %get-tuple-element.39, f32[2,2,320]{2,1,0:T(2,128)S(1)} %get-tuple-element.38), kind=kOutput, calls=%fused_computation.58 | convolution fusion | flops 107890240 | bytes 3937280 | tf_op jit(solution)/shard_map/bhqk,bqhd->bkhd/dot_general | solution.py:32
  38.3 2.8 %fusion.97 = bf16[2,320,2,128]{3,1,2,0:T(8,128)(2,1)} fusion(bf16[2,320,2,128]{3,2,1,0:T(2,128)(2,1)} %reshape.150, f32[2,2,320,320]{2,3,1,0:T(8,128)} %get-tuple-element.39, f32[2,2,320]{2,1,0:T(2,128)S(1)} %get-tuple-element.38), kind=kOutput, calls=%fused_computation.65 | convolution fusion | flops 105840640 | bytes 2298880 | tf_op jit(solution)/shard_map/bhqk,bqhd->bkhd/dot_general | solution.py:27
  43.0 2.1 fusion.247
  45.1 1.5 fusion.131
  46.6 3.8 %fusion.87 = bf16[2,320,2,128]{3,1,2,0:T(8,128)(2,1)} fusion(f32[2,2,320,320]{2,3,1,0:T(8,128)S(1)} %fusion.131, bf16[2,320,2,128]{3,2,1,0:T(2,128)(2,1)} %copy-done.23, f32[2,2,320,320]{2,3,1,0:T(8,128)} %get-tuple-element.37, f32[2,2,320]{2,1,0:T(2,128)S(1)} %get-tuple-element.36), kind=kOutput, calls=%fused_computation.61 | convolution fusion | flops 107890240 | bytes 3937280 | tf_op jit(solution)/shard_map/bhqk,bkhd->bqhd/dot_general | solution.py:31
  50.4 3.6 %fusion.84 = bf16[2,320,2,128]{3,1,2,0:T(8,128)(2,1)} fusion(f32[2,2,320,320]{2,3,1,0:T(8,128)S(1)} %fusion.131, bf16[2,320,2,128]{3,2,1,0:T(2,128)(2,1)} %copy-done.21, f32[2,2,320,320]{2,3,1,0:T(8,128)} %get-tuple-element.37, f32[2,2,320]{2,1,0:T(2,128)S(1)} %get-tuple-element.36), kind=kOutput, calls=%fused_computation.60 | convolution fusion | flops 107890240 | bytes 3937280 | tf_op jit(solution)/shard_map/bhqk,bqhd->bkhd/dot_general | solution.py:32
  54.0 2.7 %fusion.98 = bf16[2,320,2,128]{3,1,2,0:T(8,128)(2,1)} fusion(bf16[2,320,2,128]{3,2,1,0:T(2,128)(2,1)} %reshape.154, f32[2,2,320,320]{2,3,1,0:T(8,128)} %get-tuple-element.37, f32[2,2,320]{2,1,0:T(2,128)S(1)} %get-tuple-element.36), kind=kOutput, calls=%fused_computation.66 | convolution fusion | flops 105840640 | bytes 2298880 | tf_op jit(solution)/shard_map/bhqk,bqhd->bkhd/dot_general | solution.py:27
  57.0 2.3 %fusion.242 = (f32[2,2,320]{2,1,0:T(2,128)S(1)}, f32[2,2,320,320]{2,3,1,0:T(8,128)}) fusion(pred[2,320,320]{1,2,0:T(8,128)(4,1)S(1)} %fusion.124, bf16[2,320,2,128]{3,2,1,0:T(2,128)(2,1)S(1)} %reshape.157, bf16[2,320,2,128]{3,2,1,0:T(2,128)(2,1)S(1)} %reshape.156), kind=kOutput, calls=%fused_computation.203 | convolution fusion | flops 106496320 | bytes 2503680 | tf_op jit(solution)/shard_map/sub | solution.py:24
  59.8 3.6 %fusion.90 = bf16[2,320,2,128]{3,1,2,0:T(8,128)(2,1)} fusion(f32[2,2,320,320]{2,3,1,0:T(8,128)S(1)} %fusion.129, bf16[2,320,2,128]{3,2,1,0:T(2,128)(2,1)S(1)} %reshape.156, f32[2,2,320,320]{2,3,1,0:T(8,128)} %get-tuple-element.35, f32[2,2,320]{2,1,0:T(2,128)S(1)} %get-tuple-element.34), kind=kOutput, calls=%fused_computation.62 | convolution fusion | flops 107890240 | bytes 3937280 | tf_op jit(solution)/shard_map/bhqk,bqhd->bkhd/dot_general | solution.py:32
  63.4 3.7 %fusion.93 = bf16[2,320,2,128]{3,1,2,0:T(8,128)(2,1)} fusion(f32[2,2,320,320]{2,3,1,0:T(8,128)S(1)} %fusion.129, bf16[2,320,2,128]{3,2,1,0:T(2,128)(2,1)S(1)} %reshape.157, f32[2,2,320,320]{2,3,1,0:T(8,128)} %get-tuple-element.35, f32[2,2,320]{2,1,0:T(2,128)S(1)} %get-tuple-element.34), kind=kOutput, calls=%fused_computation.63 | convolution fusion | flops 107890240 | bytes 3937280 | tf_op jit(solution)/shard_map/bhqk,bkhd->bqhd/dot_general | solution.py:31
  67.1 2.7 %fusion.99 = bf16[2,320,2,128]{3,1,2,0:T(8,128)(2,1)} fusion(bf16[2,320,2,128]{3,2,1,0:T(2,128)(2,1)S(1)} %reshape.158, f32[2,2,320,320]{2,3,1,0:T(8,128)} %get-tuple-element.35, f32[2,2,320]{2,1,0:T(2,128)S(1)} %get-tuple-element.34), kind=kOutput, calls=%fused_computation.67 | convolution fusion | flops 105840640 | bytes 2298880 | tf_op jit(solution)/shard_map/bhqk,bqhd->bkhd/dot_general | solution.py:27
  75.5 2.0 copy.85
  78.7 2.0 copy.87
  80.7 1.9 stack.58
  86.1 2.0 copy.94
  88.2 1.9 stack.60
  90.1 1.7 constant_dynamic-update-slice_fusion.11
  91.8 2.0 copy.98
  93.8 1.9 stack.62
  96.4 1.7 constant_dynamic-update-slice_fusion.9
  99.6 22.9 %all_gather.7 = f32[16,3,4096]{2,1,0:T(4,128)} all-gather(f32[1,3,4096]{2,1,0:T(4,128)S(1)} %fusion.197), channel_id=1, replica_groups=mesh['section'=2,'dp'=4,'mp'=4] {'dp','mp'}, dimensions={0}, use_global_device_ids=true | all-gather | bytes 835584 | tf_op jit(solution)/shard_map/all_gather | solution.py:87
  128.3 1.4 collective-permute-start.1
  137.4 3.9 %collective-permute-done.1 = bf16[3,160,256]{2,1,0:T(8,128)(2,1)} collective-permute-done((bf16[3,160,256]{2,1,0:T(8,128)(2,1)}, bf16[3,160,256]{2,1,0:T(8,128)(2,1)}, u32[]{:S(2)}, u32[]{:S(2)}) %collective-permute-start.1) | collective-permute-done | bytes 245792 | tf_op jit(solution)/shard_map/ppermute | solution.py:82
  142.6 3.9 %collective-permute-done.2 = bf16[3,160,256]{2,1,0:T(8,128)(2,1)S(1)} collective-permute-done((bf16[3,160,256]{2,1,0:T(8,128)(2,1)}, bf16[3,160,256]{2,1,0:T(8,128)(2,1)S(1)}, u32[]{:S(2)}, u32[]{:S(2)}) %collective-permute-start.2) | collective-permute-done | bytes 245792 | tf_op jit(solution)/shard_map/ppermute | solution.py:82
  147.7 4.0 %collective-permute-done.3 = bf16[3,160,256]{2,1,0:T(8,128)(2,1)S(1)} collective-permute-done((bf16[3,160,256]{2,1,0:T(8,128)(2,1)}, bf16[3,160,256]{2,1,0:T(8,128)(2,1)S(1)}, u32[]{:S(2)}, u32[]{:S(2)}) %collective-permute-start.3) | collective-permute-done | bytes 245792 | tf_op jit(solution)/shard_map/ppermute | solution.py:82
  153.0 5.1 %collective-permute-done.4 = bf16[3,160,256]{2,1,0:T(8,128)(2,1)S(1)} collective-permute-done((bf16[3,160,256]{2,1,0:T(8,128)(2,1)}, bf16[3,160,256]{2,1,0:T(8,128)(2,1)S(1)}, u32[]{:S(2)}, u32[]{:S(2)}) %collective-permute-start.4) | collective-permute-done | bytes 245792 | tf_op jit(solution)/shard_map/ppermute | solution.py:82
  159.4 4.0 %collective-permute-done.5 = bf16[3,160,256]{2,1,0:T(8,128)(2,1)S(1)} collective-permute-done((bf16[3,160,256]{2,1,0:T(8,128)(2,1)}, bf16[3,160,256]{2,1,0:T(8,128)(2,1)S(1)}, u32[]{:S(2)}, u32[]{:S(2)}) %collective-permute-start.5) | collective-permute-done | bytes 245792 | tf_op jit(solution)/shard_map/ppermute | solution.py:82
  166.2 2.5 %collective-permute-done.6 = bf16[3,160,256]{2,1,0:T(8,128)(2,1)S(1)} collective-permute-done((bf16[3,160,256]{2,1,0:T(8,128)(2,1)S(1)}, bf16[3,160,256]{2,1,0:T(8,128)(2,1)S(1)}, u32[]{:S(2)}, u32[]{:S(2)}) %collective-permute-start.6) | collective-permute-done | bytes 245792 | tf_op jit(solution)/shard_map/ppermute | solution.py:82
  171.6 2.3 %collective-permute-done.7 = bf16[3,160,256]{2,1,0:T(8,128)(2,1)S(1)} collective-permute-done((bf16[3,160,256]{2,1,0:T(8,128)(2,1)S(1)}, bf16[3,160,256]{2,1,0:T(8,128)(2,1)S(1)}, u32[]{:S(2)}, u32[]{:S(2)}) %collective-permute-start.7) | collective-permute-done | bytes 245792 | tf_op jit(solution)/shard_map/ppermute | solution.py:82
  175.2 6.5 %collective-permute-done.8 = bf16[3,160,256]{2,1,0:T(8,128)(2,1)S(1)} collective-permute-done((bf16[3,160,256]{2,1,0:T(8,128)(2,1)S(1)}, bf16[3,160,256]{2,1,0:T(8,128)(2,1)S(1)}, u32[]{:S(2)}, u32[]{:S(2)}) %collective-permute-start.8) | collective-permute-done | bytes 245792 | tf_op jit(solution)/shard_map/ppermute | solution.py:82
  183.0 4.0 %collective-permute-done.9 = bf16[3,160,256]{2,1,0:T(8,128)(2,1)S(1)} collective-permute-done((bf16[3,160,256]{2,1,0:T(8,128)(2,1)S(1)}, bf16[3,160,256]{2,1,0:T(8,128)(2,1)S(1)}, u32[]{:S(2)}, u32[]{:S(2)}) %collective-permute-start.9) | collective-permute-done | bytes 245792 | tf_op jit(solution)/shard_map/ppermute | solution.py:82
  188.2 4.0 %collective-permute-done.10 = bf16[3,160,256]{2,1,0:T(8,128)(2,1)S(1)} collective-permute-done((bf16[3,160,256]{2,1,0:T(8,128)(2,1)S(1)}, bf16[3,160,256]{2,1,0:T(8,128)(2,1)S(1)}, u32[]{:S(2)}, u32[]{:S(2)}) %collective-permute-start.10) | collective-permute-done | bytes 245792 | tf_op jit(solution)/shard_map/ppermute | solution.py:82
  193.6 3.9 %collective-permute-done.11 = bf16[3,160,256]{2,1,0:T(8,128)(2,1)S(1)} collective-permute-done((bf16[3,160,256]{2,1,0:T(8,128)(2,1)S(1)}, bf16[3,160,256]{2,1,0:T(8,128)(2,1)S(1)}, u32[]{:S(2)}, u32[]{:S(2)}) %collective-permute-start.11) | collective-permute-done | bytes 245792 | tf_op jit(solution)/shard_map/ppermute | solution.py:82
  197.6 6.0 %collective-permute-done.12 = bf16[3,160,256]{2,1,0:T(8,128)(2,1)S(1)} collective-permute-done((bf16[3,160,256]{2,1,0:T(8,128)(2,1)S(1)}, bf16[3,160,256]{2,1,0:T(8,128)(2,1)S(1)}, u32[]{:S(2)}, u32[]{:S(2)}) %collective-permute-start.12) | collective-permute-done | bytes 245792 | tf_op jit(solution)/shard_map/ppermute | solution.py:82
  203.6 5.3 %collective-permute-done.13 = bf16[3,160,256]{2,1,0:T(8,128)(2,1)S(1)} collective-permute-done((bf16[3,160,256]{2,1,0:T(8,128)(2,1)S(1)}, bf16[3,160,256]{2,1,0:T(8,128)(2,1)S(1)}, u32[]{:S(2)}, u32[]{:S(2)}) %collective-permute-start.13) | collective-permute-done | bytes 245792 | tf_op jit(solution)/shard_map/ppermute | solution.py:82
  208.8 5.3 %collective-permute-done.14 = bf16[3,160,256]{2,1,0:T(8,128)(2,1)S(1)} collective-permute-done((bf16[3,160,256]{2,1,0:T(8,128)(2,1)S(1)}, bf16[3,160,256]{2,1,0:T(8,128)(2,1)S(1)}, u32[]{:S(2)}, u32[]{:S(2)}) %collective-permute-start.14) | collective-permute-done | bytes 245792 | tf_op jit(solution)/shard_map/ppermute | solution.py:82
  214.1 4.7 %collective-permute-done.15 = bf16[3,160,256]{2,1,0:T(8,128)(2,1)S(1)} collective-permute-done((bf16[3,160,256]{2,1,0:T(8,128)(2,1)S(1)}, bf16[3,160,256]{2,1,0:T(8,128)(2,1)S(1)}, u32[]{:S(2)}, u32[]{:S(2)}) %collective-permute-start.15) | collective-permute-done | bytes 245792 | tf_op jit(solution)/shard_map/ppermute | solution.py:82
  218.9 1.9 copy-done.1
  (140 shorter events, 51.6 us)
Async XLA Ops:
  0.6 3.2 %copy-start.10 = (bf16[1,1,640,1024]{3,2,1,0:T(8,128)(2,1)S(1)}, bf16[1,1,640,1024]{3,2,1,0:T(8,128)(2,1)}, u32[]{:S(2)}) copy-start(bf16[1,1,640,1024]{3,2,1,0:T(8,128)(2,1)} %param.6) | copy-start | bytes 3932164
  3.0 2.5 %copy-start.26 = (s32[1,1,640]{2,1,0:T(1,128)S(1)}, s32[1,1,640]{2,1,0:T(1,128)}, u32[]{:S(2)}) copy-start(s32[1,1,640]{2,1,0:T(1,128)} %param.9) | copy-start | bytes 7684
  4.8 3.9 %copy-start.11 = (bf16[1,1,640,1024]{3,2,1,0:T(8,128)(2,1)S(1)}, bf16[1,1,640,1024]{3,2,1,0:T(8,128)(2,1)}, u32[]{:S(2)}) copy-start(bf16[1,1,640,1024]{3,2,1,0:T(8,128)(2,1)} %param.7) | copy-start | bytes 3932164
  22.7 2.8 %copy-start.6 = (bf16[640,256]{1,0:T(8,128)(2,1)S(1)}, bf16[640,256]{1,0:T(8,128)(2,1)}, u32[]{:S(2)}) copy-start(bf16[640,256]{1,0:T(8,128)(2,1)} %get-tuple-element.5) | copy-start | bytes 983044
  22.7 2.9 %copy-start.7 = (bf16[640,256]{1,0:T(8,128)(2,1)S(1)}, bf16[640,256]{1,0:T(8,128)(2,1)}, u32[]{:S(2)}) copy-start(bf16[640,256]{1,0:T(8,128)(2,1)} %get-tuple-element.9) | copy-start | bytes 983044
  22.7 3.0 %copy-start.8 = (bf16[640,256]{1,0:T(8,128)(2,1)S(1)}, bf16[640,256]{1,0:T(8,128)(2,1)}, u32[]{:S(2)}) copy-start(bf16[640,256]{1,0:T(8,128)(2,1)} %get-tuple-element.13) | copy-start | bytes 983044
  25.5 1.0 copy-start.9
  25.5 1.7 copy-start.20
  25.7 1.6 copy-start.22
  38.3 2.8 %copy-start.2 = (bf16[640,256]{1,0:T(8,128)(2,1)S(1)}, bf16[640,256]{1,0:T(8,128)(2,1)}, u32[]{:S(2)}) copy-start(bf16[640,256]{1,0:T(8,128)(2,1)} %get-tuple-element.4) | copy-start | bytes 983044
  38.3 2.9 %copy-start.3 = (bf16[640,256]{1,0:T(8,128)(2,1)S(1)}, bf16[640,256]{1,0:T(8,128)(2,1)}, u32[]{:S(2)}) copy-start(bf16[640,256]{1,0:T(8,128)(2,1)} %get-tuple-element.8) | copy-start | bytes 983044
  38.3 3.0 %copy-start.4 = (bf16[640,256]{1,0:T(8,128)(2,1)S(1)}, bf16[640,256]{1,0:T(8,128)(2,1)}, u32[]{:S(2)}) copy-start(bf16[640,256]{1,0:T(8,128)(2,1)} %get-tuple-element.12) | copy-start | bytes 983044
  41.1 1.0 copy-start.5
  41.2 1.8 copy-start.21
  41.3 1.7 copy-start.23
  67.1 2.7 %copy-start.16 = (bf16[2,320,2,128]{3,1,2,0:T(8,128)(2,1)S(1)}, bf16[2,320,2,128]{3,1,2,0:T(8,128)(2,1)}, u32[]{:S(2)}) copy-start(bf16[2,320,2,128]{3,1,2,0:T(8,128)(2,1)} %fusion.75) | copy-start | bytes 983044
  69.8 1.0 copy-start.13
  69.8 1.5 copy-start.12
  71.4 1.0 copy-start.17
  72.0 1.0 copy-start.15
  72.0 1.5 copy-start.14
  73.9 1.0 copy-start.18
  82.6 1.2 copy-start.19
  123.8 10.3 %collective-permute-start.16 = (f32[3,4096]{1,0:T(4,128)S(1)}, f32[3,4096]{1,0:T(4,128)}, u32[]{:S(2)}, u32[]{:S(2)}) collective-permute-start(f32[3,4096]{1,0:T(4,128)S(1)} %reduce_sum.129), channel_id=1, source_target_pairs={{16,0},{17,1},{18,2},{19,3},{20,4},{21,5},{22,6},{23,7},{24,8},{25... | collective-permute-start | bytes 147464 | tf_op jit(solution)/shard_map/ppermute | solution.py:88
  126.0 6.0 %copy-start = (bf16[3,640,256]{2,1,0:T(8,128)(2,1)S(1)}, bf16[3,640,256]{2,1,0:T(8,128)(2,1)}, u32[]{:S(2)}) copy-start(bf16[3,640,256]{2,1,0:T(8,128)(2,1)} %constant_dynamic-update-slice_fusion.9) | copy-start | bytes 2949124
  126.0 10.1 %collective-permute-start = (bf16[3,160,256]{2,1,0:T(8,128)(2,1)S(1)}, bf16[3,160,256]{2,1,0:T(8,128)(2,1)}, u32[]{:S(2)}, u32[]{:S(2)}) collective-permute-start(bf16[3,160,256]{2,1,0:T(8,128)(2,1)S(1)} %get-tuple-element.21), channel_id=1, source_target_pairs={{16,0},{17,1},{18,2},{19,3},{20,4},{21,5},{22,6},{23,7},{24,8},{25... | collective-permute-start | bytes 737288 | tf_op jit(solution)/shard_map/ppermute | solution.py:82
  128.3 29.8 %copy-start.24 = (bf16[3,160,256]{2,1,0:T(8,128)(2,1)S(1)}, bf16[3,160,256]{2,1,0:T(8,128)(2,1)}, u32[]{:S(2)}) copy-start(bf16[3,160,256]{2,1,0:T(8,128)(2,1)} %get-tuple-element.23) | copy-start | bytes 737284
  128.3 13.0 %collective-permute-start.1 = (bf16[3,160,256]{2,1,0:T(8,128)(2,1)}, bf16[3,160,256]{2,1,0:T(8,128)(2,1)}, u32[]{:S(2)}, u32[]{:S(2)}) collective-permute-start(bf16[3,160,256]{2,1,0:T(8,128)(2,1)} %get-tuple-element.25), channel_id=1, source_target_pairs={{16,0},{17,1},{18,2},{19,3},{20,4},{21,5},{22,6},{23,7},{24,8},{25... | collective-permute-start | bytes 737288 | tf_op jit(solution)/shard_map/ppermute | solution.py:82
  130.6 10.7 %copy-start.25 = (bf16[3,160,256]{2,1,0:T(8,128)(2,1)S(1)}, bf16[3,160,256]{2,1,0:T(8,128)(2,1)}, u32[]{:S(2)}) copy-start(bf16[3,160,256]{2,1,0:T(8,128)(2,1)} %get-tuple-element.28) | copy-start | bytes 737284
  130.6 15.9 %collective-permute-start.2 = (bf16[3,160,256]{2,1,0:T(8,128)(2,1)}, bf16[3,160,256]{2,1,0:T(8,128)(2,1)S(1)}, u32[]{:S(2)}, u32[]{:S(2)}) collective-permute-start(bf16[3,160,256]{2,1,0:T(8,128)(2,1)} %get-tuple-element.29), channel_id=1, source_target_pairs={{16,0},{17,1},{18,2},{19,3},{20,4},{21,5},{22,6},{23,7},{24,8},{25... | collective-permute-start | bytes 737288 | tf_op jit(solution)/shard_map/ppermute | solution.py:82
  132.8 18.9 %collective-permute-start.3 = (bf16[3,160,256]{2,1,0:T(8,128)(2,1)}, bf16[3,160,256]{2,1,0:T(8,128)(2,1)S(1)}, u32[]{:S(2)}, u32[]{:S(2)}) collective-permute-start(bf16[3,160,256]{2,1,0:T(8,128)(2,1)} %get-tuple-element.33), channel_id=1, source_target_pairs={{16,0},{17,1},{18,2},{19,3},{20,4},{21,5},{22,6},{23,7},{24,8},{25... | collective-permute-start | bytes 737288 | tf_op jit(solution)/shard_map/ppermute | solution.py:82
  134.1 24.0 %collective-permute-start.4 = (bf16[3,160,256]{2,1,0:T(8,128)(2,1)}, bf16[3,160,256]{2,1,0:T(8,128)(2,1)S(1)}, u32[]{:S(2)}, u32[]{:S(2)}) collective-permute-start(bf16[3,160,256]{2,1,0:T(8,128)(2,1)} %get-tuple-element.20), channel_id=1, source_target_pairs={{16,1},{17,2},{18,3},{19,0},{20,5},{21,6},{22,7},{23,4},{24,9},{25... | collective-permute-start | bytes 737288 | tf_op jit(solution)/shard_map/ppermute | solution.py:82
  136.0 27.4 %collective-permute-start.5 = (bf16[3,160,256]{2,1,0:T(8,128)(2,1)}, bf16[3,160,256]{2,1,0:T(8,128)(2,1)S(1)}, u32[]{:S(2)}, u32[]{:S(2)}) collective-permute-start(bf16[3,160,256]{2,1,0:T(8,128)(2,1)} %get-tuple-element.24), channel_id=1, source_target_pairs={{16,1},{17,2},{18,3},{19,0},{20,5},{21,6},{22,7},{23,4},{24,9},{25... | collective-permute-start | bytes 737288 | tf_op jit(solution)/shard_map/ppermute | solution.py:82
  141.3 27.3 %collective-permute-start.6 = (bf16[3,160,256]{2,1,0:T(8,128)(2,1)S(1)}, bf16[3,160,256]{2,1,0:T(8,128)(2,1)S(1)}, u32[]{:S(2)}, u32[]{:S(2)}) collective-permute-start(bf16[3,160,256]{2,1,0:T(8,128)(2,1)S(1)} %copy-done.25), channel_id=1, source_target_pairs={{16,1},{17,2},{18,3},{19,0},{20,5},{21,6},{22,7},{23,4},{24,9},{25... | collective-permute-start | bytes 737288 | tf_op jit(solution)/shard_map/ppermute | solution.py:82
  146.5 27.5 %collective-permute-start.7 = (bf16[3,160,256]{2,1,0:T(8,128)(2,1)S(1)}, bf16[3,160,256]{2,1,0:T(8,128)(2,1)S(1)}, u32[]{:S(2)}, u32[]{:S(2)}) collective-permute-start(bf16[3,160,256]{2,1,0:T(8,128)(2,1)S(1)} %get-tuple-element.32), channel_id=1, source_target_pairs={{16,1},{17,2},{18,3},{19,0},{20,5},{21,6},{22,7},{23,4},{24,9},{25... | collective-permute-start | bytes 737288 | tf_op jit(solution)/shard_map/ppermute | solution.py:82
  151.7 29.9 %collective-permute-start.8 = (bf16[3,160,256]{2,1,0:T(8,128)(2,1)S(1)}, bf16[3,160,256]{2,1,0:T(8,128)(2,1)S(1)}, u32[]{:S(2)}, u32[]{:S(2)}) collective-permute-start(bf16[3,160,256]{2,1,0:T(8,128)(2,1)S(1)} %get-tuple-element.19), channel_id=1, source_target_pairs={{16,2},{17,3},{18,0},{19,1},{20,6},{21,7},{22,4},{23,5},{24,10},{2... | collective-permute-start | bytes 737288 | tf_op jit(solution)/shard_map/ppermute | solution.py:82
  158.1 28.8 %collective-permute-start.9 = (bf16[3,160,256]{2,1,0:T(8,128)(2,1)S(1)}, bf16[3,160,256]{2,1,0:T(8,128)(2,1)S(1)}, u32[]{:S(2)}, u32[]{:S(2)}) collective-permute-start(bf16[3,160,256]{2,1,0:T(8,128)(2,1)S(1)} %copy-done.24), channel_id=1, source_target_pairs={{16,2},{17,3},{18,0},{19,1},{20,6},{21,7},{22,4},{23,5},{24,10},{2... | collective-permute-start | bytes 737288 | tf_op jit(solution)/shard_map/ppermute | solution.py:82
  163.4 28.8 %collective-permute-start.10 = (bf16[3,160,256]{2,1,0:T(8,128)(2,1)S(1)}, bf16[3,160,256]{2,1,0:T(8,128)(2,1)S(1)}, u32[]{:S(2)}, u32[]{:S(2)}) collective-permute-start(bf16[3,160,256]{2,1,0:T(8,128)(2,1)S(1)} %get-tuple-element.27), channel_id=1, source_target_pairs={{16,2},{17,3},{18,0},{19,1},{20,6},{21,7},{22,4},{23,5},{24,10},{2... | collective-permute-start | bytes 737288 | tf_op jit(solution)/shard_map/ppermute | solution.py:82
  168.7 28.8 %collective-permute-start.11 = (bf16[3,160,256]{2,1,0:T(8,128)(2,1)S(1)}, bf16[3,160,256]{2,1,0:T(8,128)(2,1)S(1)}, u32[]{:S(2)}, u32[]{:S(2)}) collective-permute-start(bf16[3,160,256]{2,1,0:T(8,128)(2,1)S(1)} %get-tuple-element.31), channel_id=1, source_target_pairs={{16,2},{17,3},{18,0},{19,1},{20,6},{21,7},{22,4},{23,5},{24,10},{2... | collective-permute-start | bytes 737288 | tf_op jit(solution)/shard_map/ppermute | solution.py:82
  173.9 29.7 %collective-permute-start.12 = (bf16[3,160,256]{2,1,0:T(8,128)(2,1)S(1)}, bf16[3,160,256]{2,1,0:T(8,128)(2,1)S(1)}, u32[]{:S(2)}, u32[]{:S(2)}) collective-permute-start(bf16[3,160,256]{2,1,0:T(8,128)(2,1)S(1)} %get-tuple-element.18), channel_id=1, source_target_pairs={{16,3},{17,0},{18,1},{19,2},{20,7},{21,4},{22,5},{23,6},{24,11},{2... | collective-permute-start | bytes 737288 | tf_op jit(solution)/shard_map/ppermute | solution.py:82
  181.7 27.2 %collective-permute-start.13 = (bf16[3,160,256]{2,1,0:T(8,128)(2,1)S(1)}, bf16[3,160,256]{2,1,0:T(8,128)(2,1)S(1)}, u32[]{:S(2)}, u32[]{:S(2)}) collective-permute-start(bf16[3,160,256]{2,1,0:T(8,128)(2,1)S(1)} %get-tuple-element.22), channel_id=1, source_target_pairs={{16,3},{17,0},{18,1},{19,2},{20,7},{21,4},{22,5},{23,6},{24,11},{2... | collective-permute-start | bytes 737288 | tf_op jit(solution)/shard_map/ppermute | solution.py:82
  186.9 27.2 %collective-permute-start.14 = (bf16[3,160,256]{2,1,0:T(8,128)(2,1)S(1)}, bf16[3,160,256]{2,1,0:T(8,128)(2,1)S(1)}, u32[]{:S(2)}, u32[]{:S(2)}) collective-permute-start(bf16[3,160,256]{2,1,0:T(8,128)(2,1)S(1)} %get-tuple-element.26), channel_id=1, source_target_pairs={{16,3},{17,0},{18,1},{19,2},{20,7},{21,4},{22,5},{23,6},{24,11},{2... | collective-permute-start | bytes 737288 | tf_op jit(solution)/shard_map/ppermute | solution.py:82
  192.2 26.6 %collective-permute-start.15 = (bf16[3,160,256]{2,1,0:T(8,128)(2,1)S(1)}, bf16[3,160,256]{2,1,0:T(8,128)(2,1)S(1)}, u32[]{:S(2)}, u32[]{:S(2)}) collective-permute-start(bf16[3,160,256]{2,1,0:T(8,128)(2,1)S(1)} %get-tuple-element.30), channel_id=1, source_target_pairs={{16,3},{17,0},{18,1},{19,2},{20,7},{21,4},{22,5},{23,6},{24,11},{2... | collective-permute-start | bytes 737288 | tf_op jit(solution)/shard_map/ppermute | solution.py:82
  218.9 1.9 copy-start.1
